TPU v7x, 512 devices: a whole 4x4x16 slice. The times are simulated.
512 devices in a mesh: bond: 32 (over z, core), row: 16 (over y, x).
Axes of the slice: x: 4, y: 4, z: 16, core: 2. Of those that a mesh axis runs over, the one named last changes fastest.
Arguments:
- left_core: float32 [32, 384, 2, 384], P('bond', 'row'), may hold values from -1 to 2
- right_core: float32 [32, 384, 2, 384], P('bond', 'row'), may hold values from -1 to 2
- gate_angles: float32 [32, 6], P('bond'), may hold values from -3.140625 to 3.140625
- sketch: float32 [768, 384], P('bond'), may hold values from -0.21875 to 0.21875
Outputs:
- next_pair: float32 [32, 768, 768], P('bond', 'row')
All inputs are finite; a program needn't handle non-finite values.
Results may differ from a plain program's by a relative error of at most 0.0003.
Values sent between devices are 32-bit elements; how exact they have to be, the bound alone decides.
No kernel may reach another device: no remote copies, remote signals or barrier semaphores. Data moves between devices by JAX's collectives and lax.ppermute only.
A program may use at most 64 MiB of HBM per device.

v0:
```python
import jax
import jax.numpy as jnp
import numpy as np
from jax import lax
from jax.sharding import PartitionSpec as P

ITERS = 2
HIGHEST = lax.Precision.HIGHEST
PLANES = ((0, 1), (2, 3), (0, 2), (1, 3), (0, 3), (1, 2))


def from_behind(value, axis, steps):
    count = lax.axis_size(axis)
    initial, last = (max(0, -steps), min(count, count - steps))
    return lax.ppermute(value, axis, [(source, source + steps) for source in range(initial, last)])


def rotation(first_axis, second_axis, cosine, sine_value):
    unit = np.eye(4, dtype=np.float32)
    diag_part = np.outer(unit[first_axis], unit[first_axis]) + np.outer(
        unit[second_axis], unit[second_axis]
    )
    skew_part = np.outer(unit[second_axis], unit[first_axis]) - np.outer(
        unit[first_axis], unit[second_axis]
    )
    rest_part = np.eye(4, dtype=np.float32) - diag_part
    return (
        jnp.asarray(rest_part)
        + cosine * jnp.asarray(diag_part)
        + sine_value * jnp.asarray(skew_part)
    )


def build_gate(angles):
    gate_matrix = jnp.eye(4, dtype=jnp.float32)
    for number, plane in enumerate(PLANES):
        rotated = rotation(plane[0], plane[1], jnp.cos(angles[number]), jnp.sin(angles[number]))
        gate_matrix = jnp.dot(
            rotated, gate_matrix, precision=HIGHEST, preferred_element_type=jnp.float32
        )
    return gate_matrix


def apply_gate(two_site, gate_matrix):
    width = two_site.shape[1] // 2
    blocks = two_site.reshape(two_site.shape[0] // 2, 2, 2, width)
    mixed_gate = jnp.einsum(
        "pqtu,atuc->apqc", gate_matrix.reshape(2, 2, 2, 2), blocks, precision=HIGHEST
    )
    return mixed_gate.reshape(two_site.shape)


def matmul(left_side, right_side):
    return jnp.dot(left_side, right_side, precision=HIGHEST, preferred_element_type=jnp.float32)


def inner_rows(left_side, right_side):
    return lax.dot_general(
        left_side,
        right_side,
        (((0,), (0,)), ((), ())),
        precision=HIGHEST,
        preferred_element_type=jnp.float32,
    )


def orthonormal(sketched):
    gram_matrix = inner_rows(sketched, sketched)
    chol_factor = jnp.linalg.cholesky(gram_matrix)
    return lax.linalg.triangular_solve(
        chol_factor, sketched, left_side=False, lower=True, transpose_a=True
    )


def on_device(left_core, right_core, gate_angles, sketch):
    width = left_core.shape[3]
    local_sites = left_core.shape[1]
    local_rows = 2 * local_sites
    both = jnp.stack([left_core[0], right_core[0]], axis=1)
    both = lax.all_gather(both, "row", axis=0, tiled=True)
    sites = both.shape[0]
    left_matrix = both[:, 0].reshape(2 * sites, width)
    right_matrix = both[:, 1].reshape(sites, 2 * width)
    two_site = matmul(left_matrix, right_matrix)
    two_site = apply_gate(two_site, build_gate(gate_angles[0]))
    full_sketch = lax.all_gather(sketch, "bond", axis=0, tiled=True)
    ortho_basis = orthonormal(matmul(two_site, full_sketch))
    for repeat in range(ITERS):
        projected = inner_rows(two_site, ortho_basis)
        ortho_basis = orthonormal(matmul(two_site, projected))
    start = lax.axis_index("row") * local_sites
    my_columns = lax.dynamic_slice_in_dim(ortho_basis, start, local_sites, axis=1)
    carried = inner_rows(my_columns, two_site)
    incoming = from_behind(carried, "bond", 1)
    incoming_matrix = incoming.reshape(local_rows, width)
    next_block = matmul(incoming_matrix, ortho_basis.reshape(sites, 2 * width))
    return next_block[None]


def solution(mesh):
    return jax.shard_map(
        on_device,
        mesh=mesh,
        in_specs=(
            P("bond", "row", None, None),
            P("bond", "row", None, None),
            P("bond", None),
            P("bond", None),
        ),
        out_specs=P("bond", "row", None),
        check_vma=False,
    )
```

profile of v0, /device:TPU:1, one launch (start us, length us, event | category | flops | bytes accessed | tf_op | source)
XLA Modules:
  0.0 618.9 jit_solution(4283182410846225504)
XLA Ops:
  23.8 51.3 %all-gather.3.cloned.1.call-done = f32[384,2,2,384]{3,2,0,1:T(2,128)} async-done(((f32[24,2,2,384]{3,2,0,1:T(2,128)}), f32[384,2,2,384]{3,2,0,1:T(2,128)}) %all-gather.3.cloned.1.call-update) | async-done | bytes 2359312 | tf_op jit(solution)/shard_map/all_gather | solution.py:80
  82.4 10.3 %fusion = f32[384,384,2,2,1]{1,3,4,2,0:T(2,128)S(1)} fusion(f32[384,2,2,384,1]{3,0,2,1,4:T(8,128)S(1)} %convolution_bitcast_fusion, f32[2,2,2,2]{3,2,1,0:T(2,128)S(1)} %reshape.66), kind=kOutput, calls=%fused_computation.6 | convolution fusion | flops 28311552 | bytes 4718656 | tf_op jit(solution)/shard_map/pqtu,atuc->apqc/dot_general | solution.py:47
  92.9 56.2 %all-gather.5.cloned.1.call-done = f32[768,384]{1,0:T(8,128)} async-done(((f32[24,384]{1,0:T(8,128)}), f32[768,384]{1,0:T(8,128)}) %all-gather.5.cloned.1.call-update) | async-done | bytes 1179664 | tf_op jit(solution)/shard_map/all_gather | solution.py:86
  162.0 13.2 %cholesky.273 = f32[128,128]{1,0:T(8,128)} custom-call(f32[128,128]{1,0:T(8,128)} %cholesky.428), custom_call_target="Cholesky" | custom-call | tf_op jit(solution)/shard_map/jit(cholesky)/cholesky | solution.py:69
  178.3 20.6 %custom-call.23 = f32[1,128,128]{1,2,0:T(8,128)} custom-call(f32[1,128,128]{2,1,0:T(8,128)} %get-tuple-element.82), custom_call_target="InvertDiagBlocksLowerTriangular" | custom-call | tf_op jit(solution)/shard_map/jit(cholesky)/cholesky | solution.py:69
  203.3 13.2 %cholesky.292 = f32[128,128]{1,0:T(8,128)} custom-call(f32[128,128]{1,0:T(8,128)} %cholesky.432), custom_call_target="Cholesky" | custom-call | tf_op jit(solution)/shard_map/jit(cholesky)/cholesky | solution.py:69
  217.9 11.3 %custom-call.24 = f32[1,128,128]{1,2,0:T(8,128)} custom-call(f32[1,128,128]{2,1,0:T(8,128)} %get-tuple-element.79), custom_call_target="InvertDiagBlocksLowerTriangular" | custom-call | tf_op jit(solution)/shard_map/jit(cholesky)/cholesky | solution.py:69
  232.8 13.2 %cholesky.311 = f32[128,128]{1,0:T(8,128)} custom-call(f32[128,128]{1,0:T(8,128)} %convolution_subtract_fusion.11), custom_call_target="Cholesky" | custom-call | tf_op jit(solution)/shard_map/jit(cholesky)/cholesky | solution.py:69
  253.3 10.6 %while.6 = (s32[]{:T(128)}, f32[384,384]{1,0:T(8,128)}, s32[3,2]{0,1:T(2,128)S(1)}, f32[3,128,128]{2,1,0:T(8,128)}, s32[]{:T(128)}) while((s32[]{:T(128)}, f32[384,384]{1,0:T(8,128)}, s32[3,2]{0,1:T(2,128)S(1)}, f32[3,128,128]{2,1,0:T(8,128)}, s32[]{:T(128)}) %tuple.72), condition=%wide.while_cond, body=%wide.while_body.sunk | while | flops 2 | bytes 132205 | solution.py:70
  263.9 31.3 %custom-call.25 = f32[3,128,128]{1,2,0:T(8,128)} custom-call(f32[3,128,128]{2,1,0:T(8,128)} %get-tuple-element.27), custom_call_target="InvertDiagBlocksLowerTriangular" | custom-call | tf_op jit(solution)/shard_map/triangular_solve/custom-call.2 | solution.py:70
  321.0 13.2 %cholesky.326 = f32[128,128]{1,0:T(8,128)} custom-call(f32[128,128]{1,0:T(8,128)} %cholesky.436), custom_call_target="Cholesky" | custom-call | tf_op jit(solution)/shard_map/jit(cholesky)/cholesky | solution.py:69
  337.3 11.3 %custom-call.26 = f32[1,128,128]{1,2,0:T(8,128)} custom-call(f32[1,128,128]{2,1,0:T(8,128)} %get-tuple-element.75), custom_call_target="InvertDiagBlocksLowerTriangular" | custom-call | tf_op jit(solution)/shard_map/jit(cholesky)/cholesky | solution.py:69
  352.9 13.4 %cholesky.345 = f32[128,128]{1,0:T(8,128)} custom-call(f32[128,128]{1,0:T(8,128)} %cholesky.440), custom_call_target="Cholesky" | custom-call | tf_op jit(solution)/shard_map/jit(cholesky)/cholesky | solution.py:69
  367.7 11.3 %custom-call.27 = f32[1,128,128]{1,2,0:T(8,128)} custom-call(f32[1,128,128]{2,1,0:T(8,128)} %get-tuple-element.72), custom_call_target="InvertDiagBlocksLowerTriangular" | custom-call | tf_op jit(solution)/shard_map/jit(cholesky)/cholesky | solution.py:69
  382.6 13.2 %cholesky.364 = f32[128,128]{1,0:T(8,128)} custom-call(f32[128,128]{1,0:T(8,128)} %convolution_subtract_fusion.10), custom_call_target="Cholesky" | custom-call | tf_op jit(solution)/shard_map/jit(cholesky)/cholesky | solution.py:69
  403.8 10.6 %while.7 = (s32[]{:T(128)}, f32[384,384]{1,0:T(8,128)}, s32[3,2]{0,1:T(2,128)S(1)}, f32[3,128,128]{2,1,0:T(8,128)}, s32[]{:T(128)}) while((s32[]{:T(128)}, f32[384,384]{1,0:T(8,128)}, s32[3,2]{0,1:T(2,128)S(1)}, f32[3,128,128]{2,1,0:T(8,128)}, s32[]{:T(128)}) %tuple.85), condition=%wide.while_cond.clone, body=%wide.while_body.clone.sunk | while | flops 2 | bytes 132205 | solution.py:70
  414.3 31.3 %custom-call.28 = f32[3,128,128]{1,2,0:T(8,128)} custom-call(f32[3,128,128]{2,1,0:T(8,128)} %get-tuple-element.28), custom_call_target="InvertDiagBlocksLowerTriangular" | custom-call | tf_op jit(solution)/shard_map/triangular_solve/custom-call.2 | solution.py:70
  471.4 13.2 %cholesky.379 = f32[128,128]{1,0:T(8,128)} custom-call(f32[128,128]{1,0:T(8,128)} %cholesky.444), custom_call_target="Cholesky" | custom-call | tf_op jit(solution)/shard_map/jit(cholesky)/cholesky | solution.py:69
  487.7 11.3 %custom-call.29 = f32[1,128,128]{1,2,0:T(8,128)} custom-call(f32[1,128,128]{2,1,0:T(8,128)} %get-tuple-element.68), custom_call_target="InvertDiagBlocksLowerTriangular" | custom-call | tf_op jit(solution)/shard_map/jit(cholesky)/cholesky | solution.py:69
  503.3 13.4 %cholesky.398 = f32[128,128]{1,0:T(8,128)} custom-call(f32[128,128]{1,0:T(8,128)} %cholesky.448), custom_call_target="Cholesky" | custom-call | tf_op jit(solution)/shard_map/jit(cholesky)/cholesky | solution.py:69
  518.1 11.3 %custom-call.30 = f32[1,128,128]{1,2,0:T(8,128)} custom-call(f32[1,128,128]{2,1,0:T(8,128)} %get-tuple-element.65), custom_call_target="InvertDiagBlocksLowerTriangular" | custom-call | tf_op jit(solution)/shard_map/jit(cholesky)/cholesky | solution.py:69
  533.0 13.2 %cholesky.417 = f32[128,128]{1,0:T(8,128)} custom-call(f32[128,128]{1,0:T(8,128)} %convolution_subtract_fusion.9), custom_call_target="Cholesky" | custom-call | tf_op jit(solution)/shard_map/jit(cholesky)/cholesky | solution.py:69
  554.2 10.6 %while.8 = (s32[]{:T(128)}, f32[384,384]{1,0:T(8,128)}, s32[3,2]{0,1:T(2,128)S(1)}, f32[3,128,128]{2,1,0:T(8,128)}, s32[]{:T(128)}) while((s32[]{:T(128)}, f32[384,384]{1,0:T(8,128)}, s32[3,2]{0,1:T(2,128)S(1)}, f32[3,128,128]{2,1,0:T(8,128)}, s32[]{:T(128)}) %tuple.86), condition=%wide.while_cond.clone.1, body=%wide.while_body.clone.1.sunk | while | flops 2 | bytes 132205 | solution.py:70
  564.7 31.1 %custom-call.31 = f32[3,128,128]{1,2,0:T(8,128)} custom-call(f32[3,128,128]{2,1,0:T(8,128)} %get-tuple-element.29), custom_call_target="InvertDiagBlocksLowerTriangular" | custom-call | tf_op jit(solution)/shard_map/triangular_solve/custom-call.2 | solution.py:70
  (146 shorter events, 183.3 us)
Async XLA Ops:
  6.5 68.6 %all-gather.3.cloned.1.call-start = ((), (), s32[]{:S(2)}) async-start(), calls=%async_computation | async-start | bytes 2506752 | tf_op jit(solution)/shard_map/all_gather | solution.py:80
  8.2 141.0 %all-gather.5.cloned.1.call-start = ((), (), s32[]{:S(2)}) async-start(), calls=%async_computation.1 | async-start | bytes 1216512 | tf_op jit(solution)/shard_map/all_gather | solution.py:86
  160.5 0.8 copy-start
  202.0 0.7 copy-start.3
  295.2 3.1 copy-start.6
  319.5 0.8 copy-start.1
  351.6 0.7 copy-start.4
  445.6 3.1 copy-start.7
  469.9 0.8 copy-start.2
  502.0 0.7 copy-start.5
  595.9 3.1 copy-start.8
  604.3 4.9 collective-permute-start
Sparse Core Ops, SparseCore 0:
  10.3 64.7 all-gather.2
  77.2 71.9 all-gather.4
where the time goes:
time: 630 us; the launch traced here: 619 us
  other arithmetic  320 us (51%)
  waiting for transfers between devices  109 us (17%)
  matrix products  98.8 us (16%)
  local copies, waits for them, and re-layouts  59.9 us (10%)
  between operations  28.1 us (4%)
    another operation x32, other arithmetic, orthonormal(): chol_factor = jnp.linalg.cholesky(gram_matrix)  215 us
    another operation x8, other arithmetic, orthonormal(): lax.linalg.triangular_solve(chol_factor, sketched, left_side=False, lower...  99.6 us
    all_gather x1, waiting for transfers between devices, on_device(): full_sketch = lax.all_gather(sketch, 'bond', axis=0, tiled=True)  56.2 us
    all_gather x1, waiting for transfers between devices, on_device(): both = lax.all_gather(both, 'row', axis=0, tiled=True)  51.3 us
    another operation x32, local copies, waits for them, and re-layouts, orthonormal(): lax.linalg.triangular_solve(chol_factor, sketched, left_side=False, lower...  34.2 us
    dot_general x6, matrix products, inner_rows(): lax.dot_general(left_side, right_side, (((0,), (0,)), ((), ())), precisio...  25.5 us
    another operation x12, matrix products, orthonormal(): chol_factor = jnp.linalg.cholesky(gram_matrix)  19.9 us
    another operation x15, matrix products, orthonormal(): lax.linalg.triangular_solve(chol_factor, sketched, left_side=False, lower...  19.2 us
  transfers between devices with their start and end apart: 3, of which 3 were waited for; matrix products, arithmetic and copies ran while one was open for 4% of the time, Pallas kernels for 0%

commit v1 on v0

--- a/solution.py
+++ b/solution.py
@@ -77,7 +77,28 @@
     local_sites = left_core.shape[1]
     local_rows = 2 * local_sites
     both = jnp.stack([left_core[0], right_core[0]], axis=1)
-    both = lax.all_gather(both, "row", axis=0, tiled=True)
+    history = []
+    field_out, outer, spare = (lax.axis_size("row"), lax.axis_index("row"), both.shape[0])
+    for q in range(field_out):
+        history.append((q, (q + 1) % field_out))
+    chunks = []
+    for q in range(field_out):
+        chunks.append((q, (q - 1) % field_out))
+    opened = jnp.zeros((*both.shape[:0], field_out * spare, *both.shape[0 + 1 :]), both.dtype)
+    step_out = kept_arr = both
+    opened = lax.dynamic_update_slice_in_dim(opened, both, outer * spare, axis=0)
+    near = field_out // 2
+    for nth in range(1, near + 1):
+        step_out = lax.ppermute(step_out, "row", history)
+        opened = lax.dynamic_update_slice_in_dim(
+            opened, step_out, (outer - nth) % field_out * spare, axis=0
+        )
+        if nth < field_out - near:
+            kept_arr = lax.ppermute(kept_arr, "row", chunks)
+            opened = lax.dynamic_update_slice_in_dim(
+                opened, kept_arr, (outer + nth) % field_out * spare, axis=0
+            )
+    both = opened
     sites = both.shape[0]
     left_matrix = both[:, 0].reshape(2 * sites, width)
     right_matrix = both[:, 1].reshape(sites, 2 * width)

time: 630 us -> 590 us (0.937)
  waiting for transfers between devices: 109 us -> 18.9 us
  starting transfers between devices: 3.24 us -> 72.8 us
  other arithmetic: 320 us -> 309 us
    ppermute x0 -> x15, starting transfers between devices: none -> 63.5 us  [the longest x7 46.1 us: on_device(): kept_arr = lax.ppermute(kept_arr, 'row', chunks)]
    all_gather x1, waiting for transfers between devices: 56.2 us -> 0.02 us  [on_device(): full_sketch = lax.all_gather(sketch, 'bond', axis=0, tiled=True)]
    all_gather x1 -> x0, waiting for transfers between devices: 51.3 us -> none  [on_device(): both = lax.all_gather(both, 'row', axis=0, tiled=True)]
    ppermute x0 -> x15, waiting for transfers between devices: none -> 12.6 us  [the longest x8 12.6 us: on_device(): step_out = lax.ppermute(step_out, 'row', history)]
    another operation x32, other arithmetic: 215 us -> 206 us  [orthonormal(): chol_factor = jnp.linalg.cholesky(gram_matrix)]
  transfers between devices with their start and end apart: 3 -> 17, of which waited for: 3 -> 8; matrix products, arithmetic and copies ran while one was open for 4% -> 3% of each run, Pallas kernels for 0% -> 0%
where the time goes in v1:
time: 590 us; the launch traced here: 584 us
  other arithmetic  309 us (52%)
  matrix products  94.4 us (16%)
  starting transfers between devices  72.8 us (12%)
  local copies, waits for them, and re-layouts  59.5 us (10%)
  between operations  28.7 us (5%)
  waiting for transfers between devices  18.9 us (3%)
    another operation x32, other arithmetic, orthonormal(): chol_factor = jnp.linalg.cholesky(gram_matrix)  206 us
    another operation x8, other arithmetic, orthonormal(): lax.linalg.triangular_solve(chol_factor, sketched, left_side=False, lower...  99 us
    ppermute x7, starting transfers between devices, on_device(): kept_arr = lax.ppermute(kept_arr, 'row', chunks)  46.1 us
    another operation x32, local copies, waits for them, and re-layouts, orthonormal(): lax.linalg.triangular_solve(chol_factor, sketched, left_side=False, lower...  34.6 us
    dot_general x6, matrix products, inner_rows(): lax.dot_general(left_side, right_side, (((0,), (0,)), ((), ())), precisio...  25.5 us
    another operation x12, matrix products, orthonormal(): chol_factor = jnp.linalg.cholesky(gram_matrix)  19.8 us
    another operation x15, matrix products, orthonormal(): lax.linalg.triangular_solve(chol_factor, sketched, left_side=False, lower...  19.2 us
    dot_general x5, matrix products, matmul(): jnp.dot(left_side, right_side, precision=HIGHEST, preferred_element_type=...  18.8 us
  transfers between devices with their start and end apart: 17, of which 8 were waited for; matrix products, arithmetic and copies ran while one was open for 3% of the time, Pallas kernels for 0%

profile of v1, /device:TPU:1, one launch (start us, length us, event | category | flops | bytes accessed | tf_op | source)
XLA Modules:
  0.0 583.6 jit_solution(11031836809452026607)
XLA Ops:
  100.7 10.3 %fusion = f32[384,384,2,2,1]{1,3,4,2,0:T(2,128)S(1)} fusion(f32[384,2,2,384,1]{3,0,2,1,4:T(8,128)S(1)} %convolution_bitcast_fusion, f32[2,2,2,2]{3,2,1,0:T(2,128)S(1)} %reshape.66), kind=kOutput, calls=%fused_computation.6 | convolution fusion | flops 28311552 | bytes 4718656 | tf_op jit(solution)/shard_map/pqtu,atuc->apqc/dot_general | solution.py:47
  124.1 13.2 %cholesky.273 = f32[128,128]{1,0:T(8,128)} custom-call(f32[128,128]{1,0:T(8,128)} %cholesky.428), custom_call_target="Cholesky" | custom-call | tf_op jit(solution)/shard_map/jit(cholesky)/cholesky | solution.py:69
  140.4 11.7 %custom-call.23 = f32[1,128,128]{1,2,0:T(8,128)} custom-call(f32[1,128,128]{2,1,0:T(8,128)} %get-tuple-element.84), custom_call_target="InvertDiagBlocksLowerTriangular" | custom-call | tf_op jit(solution)/shard_map/jit(cholesky)/cholesky | solution.py:69
  156.4 13.2 %cholesky.292 = f32[128,128]{1,0:T(8,128)} custom-call(f32[128,128]{1,0:T(8,128)} %cholesky.432), custom_call_target="Cholesky" | custom-call | tf_op jit(solution)/shard_map/jit(cholesky)/cholesky | solution.py:69
  171.1 11.3 %custom-call.24 = f32[1,128,128]{1,2,0:T(8,128)} custom-call(f32[1,128,128]{2,1,0:T(8,128)} %get-tuple-element.81), custom_call_target="InvertDiagBlocksLowerTriangular" | custom-call | tf_op jit(solution)/shard_map/jit(cholesky)/cholesky | solution.py:69
  185.9 13.2 %cholesky.311 = f32[128,128]{1,0:T(8,128)} custom-call(f32[128,128]{1,0:T(8,128)} %convolution_subtract_fusion.11), custom_call_target="Cholesky" | custom-call | tf_op jit(solution)/shard_map/jit(cholesky)/cholesky | solution.py:69
  206.5 10.7 %while.6 = (s32[]{:T(128)}, f32[384,384]{1,0:T(8,128)}, s32[3,2]{0,1:T(2,128)S(1)}, f32[3,128,128]{2,1,0:T(8,128)}, s32[]{:T(128)}) while((s32[]{:T(128)}, f32[384,384]{1,0:T(8,128)}, s32[3,2]{0,1:T(2,128)S(1)}, f32[3,128,128]{2,1,0:T(8,128)}, s32[]{:T(128)}) %tuple.73), condition=%wide.while_cond, body=%wide.while_body.sunk | while | flops 2 | bytes 132205 | solution.py:70
  217.2 31.1 %custom-call.25 = f32[3,128,128]{1,2,0:T(8,128)} custom-call(f32[3,128,128]{2,1,0:T(8,128)} %get-tuple-element.27), custom_call_target="InvertDiagBlocksLowerTriangular" | custom-call | tf_op jit(solution)/shard_map/triangular_solve/custom-call.2 | solution.py:70
  254.8 7.5 %fusion.2 = f32[768,384]{1,0:T(8,128)S(1)} fusion(f32[768,768]{1,0:T(8,128)S(1)} %bitcast.182, f32[768,128]{0,1:T(8,128)S(1)} %fusion.58, f32[768,128]{0,1:T(8,128)S(1)} %fusion.59, f32[768,128]{0,1:T(8,128)S(1)} %bitcast.189), kind=kOutput, calls=%fused_computation.16 | convolution fusion | flops 2718498816 | bytes 4718592 | tf_op jit(solution)/shard_map/dot_general | solution.py:58
  274.1 13.2 %cholesky.326 = f32[128,128]{1,0:T(8,128)} custom-call(f32[128,128]{1,0:T(8,128)} %cholesky.436), custom_call_target="Cholesky" | custom-call | tf_op jit(solution)/shard_map/jit(cholesky)/cholesky | solution.py:69
  290.4 11.3 %custom-call.26 = f32[1,128,128]{1,2,0:T(8,128)} custom-call(f32[1,128,128]{2,1,0:T(8,128)} %get-tuple-element.77), custom_call_target="InvertDiagBlocksLowerTriangular" | custom-call | tf_op jit(solution)/shard_map/jit(cholesky)/cholesky | solution.py:69
  306.0 13.6 %cholesky.345 = f32[128,128]{1,0:T(8,128)} custom-call(f32[128,128]{1,0:T(8,128)} %cholesky.440), custom_call_target="Cholesky" | custom-call | tf_op jit(solution)/shard_map/jit(cholesky)/cholesky | solution.py:69
  321.1 11.3 %custom-call.27 = f32[1,128,128]{1,2,0:T(8,128)} custom-call(f32[1,128,128]{2,1,0:T(8,128)} %get-tuple-element.74), custom_call_target="InvertDiagBlocksLowerTriangular" | custom-call | tf_op jit(solution)/shard_map/jit(cholesky)/cholesky | solution.py:69
  335.9 13.2 %cholesky.364 = f32[128,128]{1,0:T(8,128)} custom-call(f32[128,128]{1,0:T(8,128)} %convolution_subtract_fusion.10), custom_call_target="Cholesky" | custom-call | tf_op jit(solution)/shard_map/jit(cholesky)/cholesky | solution.py:69
  357.1 10.7 %while.7 = (s32[]{:T(128)}, f32[384,384]{1,0:T(8,128)}, s32[3,2]{0,1:T(2,128)S(1)}, f32[3,128,128]{2,1,0:T(8,128)}, s32[]{:T(128)}) while((s32[]{:T(128)}, f32[384,384]{1,0:T(8,128)}, s32[3,2]{0,1:T(2,128)S(1)}, f32[3,128,128]{2,1,0:T(8,128)}, s32[]{:T(128)}) %tuple.84), condition=%wide.while_cond.clone, body=%wide.while_body.clone.sunk | while | flops 2 | bytes 132205 | solution.py:70
  367.8 31.1 %custom-call.28 = f32[3,128,128]{1,2,0:T(8,128)} custom-call(f32[3,128,128]{2,1,0:T(8,128)} %get-tuple-element.28), custom_call_target="InvertDiagBlocksLowerTriangular" | custom-call | tf_op jit(solution)/shard_map/triangular_solve/custom-call.2 | solution.py:70
  424.7 13.2 %cholesky.379 = f32[128,128]{1,0:T(8,128)} custom-call(f32[128,128]{1,0:T(8,128)} %cholesky.444), custom_call_target="Cholesky" | custom-call | tf_op jit(solution)/shard_map/jit(cholesky)/cholesky | solution.py:69
  441.0 11.3 %custom-call.29 = f32[1,128,128]{1,2,0:T(8,128)} custom-call(f32[1,128,128]{2,1,0:T(8,128)} %get-tuple-element.70), custom_call_target="InvertDiagBlocksLowerTriangular" | custom-call | tf_op jit(solution)/shard_map/jit(cholesky)/cholesky | solution.py:69
  456.6 13.6 %cholesky.398 = f32[128,128]{1,0:T(8,128)} custom-call(f32[128,128]{1,0:T(8,128)} %cholesky.448), custom_call_target="Cholesky" | custom-call | tf_op jit(solution)/shard_map/jit(cholesky)/cholesky | solution.py:69
  471.6 11.3 %custom-call.30 = f32[1,128,128]{1,2,0:T(8,128)} custom-call(f32[1,128,128]{2,1,0:T(8,128)} %get-tuple-element.67), custom_call_target="InvertDiagBlocksLowerTriangular" | custom-call | tf_op jit(solution)/shard_map/jit(cholesky)/cholesky | solution.py:69
  486.5 13.2 %cholesky.417 = f32[128,128]{1,0:T(8,128)} custom-call(f32[128,128]{1,0:T(8,128)} %convolution_subtract_fusion.9), custom_call_target="Cholesky" | custom-call | tf_op jit(solution)/shard_map/jit(cholesky)/cholesky | solution.py:69
  507.7 10.7 %while.8 = (s32[]{:T(128)}, f32[384,384]{1,0:T(8,128)}, s32[3,2]{0,1:T(2,128)S(1)}, f32[3,128,128]{2,1,0:T(8,128)}, s32[]{:T(128)}) while((s32[]{:T(128)}, f32[384,384]{1,0:T(8,128)}, s32[3,2]{0,1:T(2,128)S(1)}, f32[3,128,128]{2,1,0:T(8,128)}, s32[]{:T(128)}) %tuple.85), condition=%wide.while_cond.clone.1, body=%wide.while_body.clone.1.sunk | while | flops 2 | bytes 132205 | solution.py:70
  518.4 31.1 %custom-call.31 = f32[3,128,128]{1,2,0:T(8,128)} custom-call(f32[3,128,128]{2,1,0:T(8,128)} %get-tuple-element.29), custom_call_target="InvertDiagBlocksLowerTriangular" | custom-call | tf_op jit(solution)/shard_map/triangular_solve/custom-call.2 | solution.py:70
  557.9 9.3 %collective-permute-start.15 = (f32[24,768]{1,0:T(8,128)}, f32[24,768]{1,0:T(8,128)}, u32[]{:S(2)}, u32[]{:S(2)}) collective-permute-start(f32[24,768]{1,0:T(8,128)} %fusion.46), channel_id=1, source_target_pairs={{0,16},{16,32},{32,48},{48,64},{64,80},{80,96},{96,112},{112,128},... | collective-permute-start | bytes 221192 | tf_op jit(solution)/shard_map/ppermute | solution.py:15
  (219 shorter events, 247.2 us)
Async XLA Ops:
  6.5 104.7 %all-gather.2.cloned.1.call-start = ((), (), s32[]{:S(2)}) async-start(), calls=%async_computation | async-start | bytes 1216512 | tf_op jit(solution)/shard_map/all_gather | solution.py:107
  6.6 19.9 %copy-start.14 = (f32[4,4]{1,0:T(4,128)S(1)}, f32[4,4]{1,0:T(4,128)}, u32[]{:S(2)}) copy-start(f32[4,4]{1,0:T(4,128)} %constant.217.clone) | copy-start | bytes 196
  6.6 19.9 %copy-start.15 = (f32[4,4]{1,0:T(4,128)S(1)}, f32[4,4]{1,0:T(4,128)}, u32[]{:S(2)}) copy-start(f32[4,4]{1,0:T(4,128)} %constant.218.clone) | copy-start | bytes 196
  6.6 20.0 %copy-start.20 = (f32[4,4]{1,0:T(4,128)S(1)}, f32[4,4]{1,0:T(4,128)}, u32[]{:S(2)}) copy-start(f32[4,4]{1,0:T(4,128)} %constant.220.clone) | copy-start | bytes 196
  6.6 20.1 %copy-start.12 = (f32[4,4]{1,0:T(4,128)S(1)}, f32[4,4]{1,0:T(4,128)}, u32[]{:S(2)}) copy-start(f32[4,4]{1,0:T(4,128)} %constant.221.clone) | copy-start | bytes 196
  6.7 20.1 %copy-start.13 = (f32[4,4]{1,0:T(4,128)S(1)}, f32[4,4]{1,0:T(4,128)}, u32[]{:S(2)}) copy-start(f32[4,4]{1,0:T(4,128)} %constant.222.clone) | copy-start | bytes 196
  6.7 20.1 %copy-start.19 = (f32[4,4]{1,0:T(4,128)S(1)}, f32[4,4]{1,0:T(4,128)}, u32[]{:S(2)}) copy-start(f32[4,4]{1,0:T(4,128)} %constant.223.clone) | copy-start | bytes 196
  6.7 20.2 %copy-start.18 = (f32[4,4]{1,0:T(4,128)S(1)}, f32[4,4]{1,0:T(4,128)}, u32[]{:S(2)}) copy-start(f32[4,4]{1,0:T(4,128)} %constant.224.clone) | copy-start | bytes 196
  7.6 19.7 %collective-permute-start = (f32[24,2,2,384]{3,2,0,1:T(2,128)S(1)}, f32[24,2,2,384]{3,2,0,1:T(2,128)S(1)}, u32[]{:S(2)}, u32[]{:S(2)}) collective-permute-start(f32[24,2,2,384]{3,2,0,1:T(2,128)S(1)} %get-tuple-element.62), channel_id=1, source_target_pairs={{0,1},{1,2},{2,3},{3,4},{4,5},{5,6},{6,7},{7,8},{8,9},{9,10},{10,1... | collective-permute-start | bytes 442376 | tf_op jit(solution)/shard_map/ppermute | solution.py:92
  11.5 17.7 %collective-permute-start.1 = (f32[24,2,2,384]{3,2,0,1:T(2,128)S(1)}, f32[24,2,2,384]{3,2,0,1:T(2,128)S(1)}, u32[]{:S(2)}, u32[]{:S(2)}) collective-permute-start(f32[24,2,2,384]{3,2,0,1:T(2,128)S(1)} %get-tuple-element.62), channel_id=1, source_target_pairs={{0,15},{1,0},{2,1},{3,2},{4,3},{5,4},{6,5},{7,6},{8,7},{9,8},{10,9... | collective-permute-start | bytes 442376 | tf_op jit(solution)/shard_map/ppermute | solution.py:97
  27.3 9.2 %collective-permute-start.2 = (f32[24,2,2,384]{3,2,0,1:T(2,128)S(1)}, f32[24,2,2,384]{3,2,0,1:T(2,128)S(1)}, u32[]{:S(2)}, u32[]{:S(2)}) collective-permute-start(f32[24,2,2,384]{3,2,0,1:T(2,128)S(1)} %collective-permute-done), channel_id=1, source_target_pairs={{0,1},{1,2},{2,3},{3,4},{4,5},{5,6},{6,7},{7,8},{8,9},{9,10},{10,1... | collective-permute-start | bytes 442376 | tf_op jit(solution)/shard_map/ppermute | solution.py:92
  29.3 9.2 %collective-permute-start.3 = (f32[24,2,2,384]{3,2,0,1:T(2,128)S(1)}, f32[24,2,2,384]{3,2,0,1:T(2,128)S(1)}, u32[]{:S(2)}, u32[]{:S(2)}) collective-permute-start(f32[24,2,2,384]{3,2,0,1:T(2,128)S(1)} %collective-permute-done.1), channel_id=1, source_target_pairs={{0,15},{1,0},{2,1},{3,2},{4,3},{5,4},{6,5},{7,6},{8,7},{9,8},{10,9... | collective-permute-start | bytes 442376 | tf_op jit(solution)/shard_map/ppermute | solution.py:97
  36.5 9.2 %collective-permute-start.4 = (f32[24,2,2,384]{3,2,0,1:T(2,128)S(1)}, f32[24,2,2,384]{3,2,0,1:T(2,128)S(1)}, u32[]{:S(2)}, u32[]{:S(2)}) collective-permute-start(f32[24,2,2,384]{3,2,0,1:T(2,128)S(1)} %collective-permute-done.2), channel_id=1, source_target_pairs={{0,1},{1,2},{2,3},{3,4},{4,5},{5,6},{6,7},{7,8},{8,9},{9,10},{10,1... | collective-permute-start | bytes 442376 | tf_op jit(solution)/shard_map/ppermute | solution.py:92
  38.5 9.2 %collective-permute-start.5 = (f32[24,2,2,384]{3,2,0,1:T(2,128)S(1)}, f32[24,2,2,384]{3,2,0,1:T(2,128)S(1)}, u32[]{:S(2)}, u32[]{:S(2)}) collective-permute-start(f32[24,2,2,384]{3,2,0,1:T(2,128)S(1)} %collective-permute-done.3), channel_id=1, source_target_pairs={{0,15},{1,0},{2,1},{3,2},{4,3},{5,4},{6,5},{7,6},{8,7},{9,8},{10,9... | collective-permute-start | bytes 442376 | tf_op jit(solution)/shard_map/ppermute | solution.py:97
  45.7 9.6 %collective-permute-start.6 = (f32[24,2,2,384]{3,2,0,1:T(2,128)S(1)}, f32[24,2,2,384]{3,2,0,1:T(2,128)S(1)}, u32[]{:S(2)}, u32[]{:S(2)}) collective-permute-start(f32[24,2,2,384]{3,2,0,1:T(2,128)S(1)} %collective-permute-done.4), channel_id=1, source_target_pairs={{0,1},{1,2},{2,3},{3,4},{4,5},{5,6},{6,7},{7,8},{8,9},{9,10},{10,1... | collective-permute-start | bytes 442376 | tf_op jit(solution)/shard_map/ppermute | solution.py:92
  47.6 9.6 %collective-permute-start.7 = (f32[24,2,2,384]{3,2,0,1:T(2,128)S(1)}, f32[24,2,2,384]{3,2,0,1:T(2,128)S(1)}, u32[]{:S(2)}, u32[]{:S(2)}) collective-permute-start(f32[24,2,2,384]{3,2,0,1:T(2,128)S(1)} %collective-permute-done.5), channel_id=1, source_target_pairs={{0,15},{1,0},{2,1},{3,2},{4,3},{5,4},{6,5},{7,6},{8,7},{9,8},{10,9... | collective-permute-start | bytes 442376 | tf_op jit(solution)/shard_map/ppermute | solution.py:97
  55.3 11.0 %collective-permute-start.8 = (f32[24,2,2,384]{3,2,0,1:T(2,128)S(1)}, f32[24,2,2,384]{3,2,0,1:T(2,128)S(1)}, u32[]{:S(2)}, u32[]{:S(2)}) collective-permute-start(f32[24,2,2,384]{3,2,0,1:T(2,128)S(1)} %collective-permute-done.6), channel_id=1, source_target_pairs={{0,1},{1,2},{2,3},{3,4},{4,5},{5,6},{6,7},{7,8},{8,9},{9,10},{10,1... | collective-permute-start | bytes 442376 | tf_op jit(solution)/shard_map/ppermute | solution.py:92
  57.3 11.0 %collective-permute-start.9 = (f32[24,2,2,384]{3,2,0,1:T(2,128)S(1)}, f32[24,2,2,384]{3,2,0,1:T(2,128)S(1)}, u32[]{:S(2)}, u32[]{:S(2)}) collective-permute-start(f32[24,2,2,384]{3,2,0,1:T(2,128)S(1)} %collective-permute-done.7), channel_id=1, source_target_pairs={{0,15},{1,0},{2,1},{3,2},{4,3},{5,4},{6,5},{7,6},{8,7},{9,8},{10,9... | collective-permute-start | bytes 442376 | tf_op jit(solution)/shard_map/ppermute | solution.py:97
  66.4 10.2 %collective-permute-start.10 = (f32[24,2,2,384]{3,2,0,1:T(2,128)S(1)}, f32[24,2,2,384]{3,2,0,1:T(2,128)S(1)}, u32[]{:S(2)}, u32[]{:S(2)}) collective-permute-start(f32[24,2,2,384]{3,2,0,1:T(2,128)S(1)} %collective-permute-done.8), channel_id=1, source_target_pairs={{0,1},{1,2},{2,3},{3,4},{4,5},{5,6},{6,7},{7,8},{8,9},{9,10},{10,1... | collective-permute-start | bytes 442376 | tf_op jit(solution)/shard_map/ppermute | solution.py:92
  68.3 10.2 %collective-permute-start.11 = (f32[24,2,2,384]{3,2,0,1:T(2,128)S(1)}, f32[24,2,2,384]{3,2,0,1:T(2,128)S(1)}, u32[]{:S(2)}, u32[]{:S(2)}) collective-permute-start(f32[24,2,2,384]{3,2,0,1:T(2,128)S(1)} %collective-permute-done.9), channel_id=1, source_target_pairs={{0,15},{1,0},{2,1},{3,2},{4,3},{5,4},{6,5},{7,6},{8,7},{9,8},{10,9... | collective-permute-start | bytes 442376 | tf_op jit(solution)/shard_map/ppermute | solution.py:97
  76.6 9.2 %collective-permute-start.12 = (f32[24,2,2,384]{3,2,0,1:T(2,128)S(1)}, f32[24,2,2,384]{3,2,0,1:T(2,128)S(1)}, u32[]{:S(2)}, u32[]{:S(2)}) collective-permute-start(f32[24,2,2,384]{3,2,0,1:T(2,128)S(1)} %collective-permute-done.10), channel_id=1, source_target_pairs={{0,1},{1,2},{2,3},{3,4},{4,5},{5,6},{6,7},{7,8},{8,9},{9,10},{10,1... | collective-permute-start | bytes 442376 | tf_op jit(solution)/shard_map/ppermute | solution.py:92
  78.5 9.4 %collective-permute-start.13 = (f32[24,2,2,384]{3,2,0,1:T(2,128)S(1)}, f32[24,2,2,384]{3,2,0,1:T(2,128)S(1)}, u32[]{:S(2)}, u32[]{:S(2)}) collective-permute-start(f32[24,2,2,384]{3,2,0,1:T(2,128)S(1)} %collective-permute-done.11), channel_id=1, source_target_pairs={{0,15},{1,0},{2,1},{3,2},{4,3},{5,4},{6,5},{7,6},{8,7},{9,8},{10,9... | collective-permute-start | bytes 442376 | tf_op jit(solution)/shard_map/ppermute | solution.py:97
  85.8 9.2 %collective-permute-start.14 = (f32[24,2,2,384]{3,2,0,1:T(2,128)S(1)}, f32[24,2,2,384]{3,2,0,1:T(2,128)S(1)}, u32[]{:S(2)}, u32[]{:S(2)}) collective-permute-start(f32[24,2,2,384]{3,2,0,1:T(2,128)S(1)} %collective-permute-done.12), channel_id=1, source_target_pairs={{0,1},{1,2},{2,3},{3,4},{4,5},{5,6},{6,7},{7,8},{8,9},{9,10},{10,1... | collective-permute-start | bytes 442376 | tf_op jit(solution)/shard_map/ppermute | solution.py:92
  557.9 16.3 %collective-permute-start.15 = (f32[24,768]{1,0:T(8,128)}, f32[24,768]{1,0:T(8,128)}, u32[]{:S(2)}, u32[]{:S(2)}) collective-permute-start(f32[24,768]{1,0:T(8,128)} %fusion.46), channel_id=1, source_target_pairs={{0,16},{16,32},{32,48},{48,64},{64,80},{80,96},{96,112},{112,128},... | collective-permute-start | bytes 221192 | tf_op jit(solution)/shard_map/ppermute | solution.py:15
  (17 other events, 124.6 us)
Sparse Core Ops, SparseCore 0:
  17.3 72.5 all-gather.1
